TPU v7x, 512 devices: a whole 4x4x16 slice. The times are simulated.
512 devices in a mesh: xb: 16 (over x, y), zs: 32 (over z, core).
Axes of the slice: x: 4, y: 4, z: 16, core: 2. Of those that a mesh axis runs over, the one named last changes fastest.
Arguments:
- partials: bfloat16 [16384, 32768], P(('xb', 'zs')), may hold values from -6 to 6
- routes: int32 [512, 32], P(('xb', 'zs')), may hold values from 0 to 255, as said below
- taps: float32 [3, 129], replicated, may hold values from 0.25 to 2.5
Outputs:
- gradient: float32 [1024, 1024, 128], P('xb', 'zs')
- smoothed: float32 [1024, 1024, 128], P('xb', 'zs')
Inputs may be any that keep to these rules, and one draw needn't show every extreme that they name: `routes`: an entry v of a device's list names local block v % (8) of the device with zs index v // 8 in the same xb group; the entries of one list that name the same owner all name the same block, and no owner is named by more than two entries of one list.
All inputs are finite; a program needn't handle non-finite values.
Results may differ from a plain program's by a relative error of at most 0.0077.
Values may be sent and summed in bfloat16 or wider, within the bound.
No kernel may reach another device: no remote copies, remote signals or barrier semaphores. Data moves between devices by JAX's collectives and lax.ppermute only.
A program may use at most 64 MiB of HBM per device.

v0:
```python
import jax
import jax.numpy as jnp
from jax import lax
from jax.sharding import PartitionSpec as P

BLK = 32
YBLOCKS = 4
CELLS = 32768
CX = 64
CZ = 32
REACH = 64
NY = 128


def extended_2(x, sides, width):
    for axis, dim in sides:
        count, length = (lax.axis_size(axis), x.shape[dim])
        up = [(i, (i + 1) % count) for i in range(count - 1)]
        down = [(j, i) for i, j in up]
        last = lax.slice_in_dim(x, length - width, length, axis=dim)
        initial = lax.slice_in_dim(x, 0, width, axis=dim)
        before = lax.ppermute(last, axis, up)
        after = lax.ppermute(initial, axis, down)
        x = jnp.concatenate([before, x, after], axis=dim)
    return x


def band_matrix(kern_row, rows, cols, offset):
    border = rows + cols
    widened = jnp.pad(kern_row, ((border, border),))
    front = widened[offset + border : offset + border + cols]
    behind = widened[offset + border - rows : offset + border]
    cycle = jnp.concatenate([front, behind])
    period = rows + cols - 1
    tiled = jnp.tile(cycle, rows)[: rows * period]
    return tiled.reshape(rows, period)[:, :cols]


def body(partials, routes, taps):
    owners_count = lax.axis_size("zs")
    blocks_local = 2 * YBLOCKS
    entries = routes[0]
    owner = entries // blocks_local
    block_id = entries % blocks_local
    owner_hit = owner[:, None] == jnp.arange(owners_count)[None, :]
    hit_count = owner_hit.astype(jnp.int32)
    earlier = jnp.cumsum(hit_count, axis=0) - hit_count
    rank = jnp.sum(earlier * hit_count, axis=1)
    target = owner * 2 + rank
    select = target[None, :] == jnp.arange(2 * owners_count)[:, None]
    packed = jnp.dot(select.astype(jnp.bfloat16), partials, preferred_element_type=jnp.float32)
    packed = packed.astype(jnp.bfloat16).reshape(owners_count, 2, CELLS)
    packed_ids = jnp.sum(jnp.where(select, block_id[None, :], 0), axis=1).reshape(owners_count, 2)
    arrived, arrived_ids = (
        lax.all_to_all(packed, "zs", split_axis=0, concat_axis=0, tiled=True),
        lax.all_to_all(packed_ids, "zs", split_axis=0, concat_axis=0, tiled=True),
    )
    contrib = (arrived[:, 0].astype(jnp.float32) + arrived[:, 1].astype(jnp.float32)).astype(
        jnp.bfloat16
    )
    source_ids = arrived_ids[:, 0]
    placing = (source_ids[None, :] == jnp.arange(blocks_local)[:, None]).astype(jnp.bfloat16)
    assembled = jnp.dot(placing, contrib, preferred_element_type=jnp.float32)
    assembled = assembled.reshape(2, YBLOCKS, BLK, BLK, BLK).transpose(0, 2, 4, 1, 3)
    gradient = assembled.reshape(CX, CZ, NY)
    norms = jnp.sqrt(jnp.sum(taps * taps, axis=1, keepdims=True))
    kernel = (taps / norms).astype(jnp.bfloat16)
    field = gradient.astype(jnp.bfloat16)
    padded = extended_2(field, (("xb", 0),), CX)
    x_matrix = band_matrix(kernel[0], CX, 3 * CX, 0)
    along_x = jnp.dot(x_matrix, padded.reshape(3 * CX, CZ * NY), preferred_element_type=jnp.float32)
    along_x = along_x.astype(jnp.bfloat16).reshape(CX, CZ, NY)
    y_matrix = band_matrix(kernel[1], NY, NY, REACH)
    along_y = jnp.einsum(
        "ab,xzb->xza", y_matrix, along_x, preferred_element_type=jnp.float32
    ).astype(jnp.bfloat16)
    line_length = CZ * owners_count
    columns = CX * NY // owners_count
    z_major = along_y.transpose(1, 0, 2).reshape(CZ, owners_count, columns)
    z_matrix = band_matrix(kernel[2], REACH, 3 * REACH, 0)
    lines = lax.all_to_all(z_major, "zs", split_axis=1, concat_axis=0, tiled=True)
    flat = lines.reshape(line_length, lines.shape[2])
    extended = jnp.pad(flat, ((REACH, REACH), (0, 0)))
    pieces = extended.reshape(line_length // REACH + 2, REACH, flat.shape[1])
    windows = jnp.concatenate([pieces[:-2], pieces[1:-1], pieces[2:]], axis=1)
    filtered = jnp.einsum("ij,bjm->bim", z_matrix, windows, preferred_element_type=jnp.float32)
    filtered = filtered.reshape(line_length, 1, flat.shape[1])
    returned = lax.all_to_all(filtered, "zs", split_axis=0, concat_axis=1, tiled=True)
    smoothed = returned.reshape(CZ, CX, NY).transpose(1, 0, 2)
    return (gradient, smoothed)


def solution(mesh):
    placed = (P(("xb", "zs"), None), P(("xb", "zs"), None), P())
    return jax.shard_map(
        body,
        mesh=mesh,
        in_specs=placed,
        out_specs=(P("xb", "zs", None), P("xb", "zs", None)),
        check_vma=False,
    )
```

profile of v0, /device:TPU:26, one launch (start us, length us, event | category | flops | bytes accessed | tf_op | source)
XLA Modules:
  0.0 409.5 jit_solution(13148397627251615303)
XLA Ops:
  0.6 0.0 copy-start
  0.6 0.8 and_select_fusion.1
  1.5 0.1 fusion.14
  1.5 0.1 reduce_window_sum.11
  1.6 0.2 select_reduce_fusion.1
  1.8 0.7 fusion.20
  2.4 0.1 select_reduce_fusion
  2.5 0.7 all_to_all.33
  3.3 15.5 %all-to-all-start = ((s32[32,1,2]{2,1,0:T(1,128)}), s32[32,1,2]{2,1,0:T(1,128)S(1)}, u32[]{:S(2)}, u32[]{:S(2)}) async-start(s32[32,1,2]{2,1,0:T(1,128)} %bitcast.4), calls=%async_computation | async-start | bytes 32768 | tf_op jit(solution)/shard_map/all_to_all | solution.py:56
  18.7 0.0 copy-done
  18.8 3.3 convolution_convert_fusion
  22.1 7.6 %reshape.109 = bf16[32,2,32768]{2,1,0:T(2,128)(2,1)} reshape(bf16[64,32768]{1,0:T(8,128)(2,1)} %convolution_convert_fusion) | data formatting | bytes 8388608 | tf_op jit(solution)/shard_map/reshape | solution.py:52
  29.7 0.0 copy-start.2
  29.7 1.4 all-to-all-done
  31.1 11.2 %all-to-all-start.1 = ((bf16[32,2,32768]{2,1,0:T(2,128)(2,1)}), bf16[32,2,32768]{2,1,0:T(2,128)(2,1)}, u32[]{:S(2)}, u32[]{:S(2)}) async-start(bf16[32,2,32768]{2,1,0:T(2,128)(2,1)} %reshape.109), calls=%async_computation.1 | async-start | bytes 8388608 | tf_op jit(solution)/shard_map/all_to_all | solution.py:55
  42.3 0.0 copy-done.2
  42.3 0.1 multiply_reduce_fusion
  42.5 0.1 divide_convert_fusion
  42.6 0.1 copy.35
  42.7 183.2 %all-to-all-done.1 = bf16[32,2,32768]{2,1,0:T(2,128)(2,1)} async-done(((bf16[32,2,32768]{2,1,0:T(2,128)(2,1)}), bf16[32,2,32768]{2,1,0:T(2,128)(2,1)}, u32[]{:S(2)}, u32[]{:S(2)}) %all-to-all-start.1) | async-done | bytes 4194336 | tf_op jit(solution)/shard_map/all_to_all | solution.py:55
  225.9 9.0 %fusion.23 = (bf16[32,1,32768]{2,1,0:T(2,128)(2,1)S(1)}, bf16[32,1,32768]{2,1,0:T(2,128)(2,1)S(1)}) fusion(bf16[32,2,32768]{2,1,0:T(2,128)(2,1)} %all-to-all-done.1), kind=kLoop, calls=%fused_computation.61 | loop fusion | bytes 8388608 | tf_op jit(solution)/shard_map/slice | solution.py:58
  234.9 5.9 %fusion = bf16[32768,32]{0,1:T(8,128)(2,1)} fusion(bf16[32,1,32768]{2,1,0:T(2,128)(2,1)S(1)} %get-tuple-element.14, bf16[32,1,32768]{2,1,0:T(2,128)(2,1)S(1)} %get-tuple-element.13), kind=kLoop, calls=%fused_computation.4 | loop fusion | flops 4194304 | bytes 6291456 | tf_op jit(solution)/shard_map/dot_general | solution.py:63
  240.8 7.4 %copy.46 = bf16[32768,32]{1,0:T(8,128)(2,1)} copy(bf16[32768,32]{0,1:T(8,128)(2,1)} %fusion) | data formatting | bytes 4194304 | tf_op jit(solution)/shard_map/dot_general | solution.py:63
  248.1 16.3 %convolution_bitcast_fusion = f32[2,32,32,4,32]{2,3,4,1,0:T(4,128)} fusion(bf16[32,32,32,32,1]{3,2,1,0,4:T(8,128)(2,1)} %bitcast.86, s32[2,4]{1,0:T(2,128)S(1)} %multiply_add_fusion, s32[32]{0:T(128)S(1)} %slice_bitcast_fusion.4), kind=kOutput, calls=%fused_computation.3 | convolution fusion | flops 16777472 | bytes 3145888 | tf_op jit(solution)/shard_map/dot_general | solution.py:63
  264.4 6.3 %copy.39 = f32[2,32,32,4,32]{4,3,2,1,0:T(4,128)} copy(f32[2,32,32,4,32]{2,3,4,1,0:T(4,128)} %convolution_bitcast_fusion) | data formatting | bytes 2097152 | tf_op jit(solution)/shard_map/transpose | solution.py:64
  270.7 3.7 reshape.110
  274.4 0.0 copy-start.1
  274.4 1.0 convert_element_type.51
  275.5 3.0 collective-permute-start
  278.5 3.0 collective-permute-start.1
  281.6 0.2 reshape.111
  281.8 0.1 pad_slice_fusion.3
  281.9 0.1 copy.54
  282.0 0.3 reshape.114
  282.3 8.9 %collective-permute-done = bf16[64,32,128]{2,1,0:T(8,128)(2,1)} collective-permute-done((bf16[64,32,128]{2,1,0:T(8,128)(2,1)}, bf16[64,32,128]{2,1,0:T(8,128)(2,1)}, u32[]{:S(2)}, u32[]{:S(2)}) %collective-permute-start) | collective-permute-done | bytes 524320 | tf_op jit(solution)/shard_map/ppermute | solution.py:22
  291.2 4.9 %collective-permute-done.1 = bf16[64,32,128]{2,1,0:T(8,128)(2,1)} collective-permute-done((bf16[64,32,128]{2,1,0:T(8,128)(2,1)}, bf16[64,32,128]{2,1,0:T(8,128)(2,1)}, u32[]{:S(2)}, u32[]{:S(2)}) %collective-permute-start.1) | collective-permute-done | bytes 524320 | tf_op jit(solution)/shard_map/ppermute | solution.py:23
  296.1 1.5 pad_maximum_fusion
  297.6 0.6 fusion.10
  298.3 0.0 copy-done.1
  298.3 0.1 copy.53
  298.4 0.3 fusion.9
  298.7 0.2 copy.40
  298.9 0.2 reshape.115
  299.1 1.1 copy.41
  300.1 9.9 %all-to-all-start.2 = ((bf16[32,32,256]{2,0,1:T(8,128)(2,1)}), bf16[32,32,256]{2,0,1:T(8,128)(2,1)S(1)}, u32[]{:S(2)}, u32[]{:S(2)}) async-start(bf16[32,32,256]{2,0,1:T(8,128)(2,1)} %copy.41), calls=%async_computation.2 | async-start | bytes 1048576 | tf_op jit(solution)/shard_map/all_to_all | solution.py:81
  310.2 0.2 reshape.117
  310.3 33.5 %all-to-all-done.2 = bf16[32,32,256]{2,0,1:T(8,128)(2,1)S(1)} async-done(((bf16[32,32,256]{2,0,1:T(8,128)(2,1)}), bf16[32,32,256]{2,0,1:T(8,128)(2,1)S(1)}, u32[]{:S(2)}, u32[]{:S(2)}) %all-to-all-start.2) | async-done | bytes 524320 | tf_op jit(solution)/shard_map/all_to_all | solution.py:81
  343.9 0.1 pad_slice_fusion.1
  343.9 0.4 fusion.3
  344.3 1.1 copy.42
  345.4 59.5 %all_to_all.47 = f32[1024,1,256]{2,1,0:T(1,128)S(1)} all-to-all(f32[1024,1,256]{2,1,0:T(1,128)S(1)} %copy.42), channel_id=1, replica_groups=mesh['xb'=16,'zs'=32] {'zs'}, dimensions={0} | all-to-all | bytes 2097152 | tf_op jit(solution)/shard_map/all_to_all | solution.py:88
  404.9 0.1 copy.47
  405.0 0.6 copy.43
  405.6 1.1 reshape.119
  406.7 2.8 copy.44
  (13 shorter events, 0.2 us)
Async XLA Ops:
  0.6 18.1 %copy-start = (bf16[32,32768]{1,0:T(8,128)(2,1)S(1)}, bf16[32,32768]{1,0:T(8,128)(2,1)}, u32[]{:S(2)}) copy-start(bf16[32,32768]{1,0:T(8,128)(2,1)} %param.3) | copy-start | bytes 6291460
  3.3 27.9 %all-to-all-start = ((s32[32,1,2]{2,1,0:T(1,128)}), s32[32,1,2]{2,1,0:T(1,128)S(1)}, u32[]{:S(2)}, u32[]{:S(2)}) async-start(s32[32,1,2]{2,1,0:T(1,128)} %bitcast.4), calls=%async_computation | async-start | bytes 32768 | tf_op jit(solution)/shard_map/all_to_all | solution.py:56
  29.7 12.6 %copy-start.2 = (f32[3,129]{1,0:T(4,128)S(1)}, f32[3,129]{1,0:T(4,128)}, u32[]{:S(2)}) copy-start(f32[3,129]{1,0:T(4,128)} %param.5) | copy-start | bytes 4648
  31.1 194.8 %all-to-all-start.1 = ((bf16[32,2,32768]{2,1,0:T(2,128)(2,1)}), bf16[32,2,32768]{2,1,0:T(2,128)(2,1)}, u32[]{:S(2)}, u32[]{:S(2)}) async-start(bf16[32,2,32768]{2,1,0:T(2,128)(2,1)} %reshape.109), calls=%async_computation.1 | async-start | bytes 8388608 | tf_op jit(solution)/shard_map/all_to_all | solution.py:55
  274.4 23.8 %copy-start.1 = (f32[64,32,128]{2,1,0:T(8,128)}, f32[64,32,128]{2,1,0:T(8,128)S(1)}, u32[]{:S(2)}) copy-start(f32[64,32,128]{2,1,0:T(8,128)S(1)} %reshape.110) | copy-start | bytes 3145732
  275.5 15.7 %collective-permute-start = (bf16[64,32,128]{2,1,0:T(8,128)(2,1)}, bf16[64,32,128]{2,1,0:T(8,128)(2,1)}, u32[]{:S(2)}, u32[]{:S(2)}) collective-permute-start(bf16[64,32,128]{2,1,0:T(8,128)(2,1)} %convert_element_type.51), channel_id=1, source_target_pairs={{0,32},{32,64},{64,96},{96,128},{128,160},{160,192},{192,224},{224... | collective-permute-start | bytes 1572872 | tf_op jit(solution)/shard_map/ppermute | solution.py:22
  278.5 17.5 %collective-permute-start.1 = (bf16[64,32,128]{2,1,0:T(8,128)(2,1)}, bf16[64,32,128]{2,1,0:T(8,128)(2,1)}, u32[]{:S(2)}, u32[]{:S(2)}) collective-permute-start(bf16[64,32,128]{2,1,0:T(8,128)(2,1)} %convert_element_type.51), channel_id=1, source_target_pairs={{32,0},{64,32},{96,64},{128,96},{160,128},{192,160},{224,192},{256... | collective-permute-start | bytes 1572872 | tf_op jit(solution)/shard_map/ppermute | solution.py:23
  300.1 43.7 %all-to-all-start.2 = ((bf16[32,32,256]{2,0,1:T(8,128)(2,1)}), bf16[32,32,256]{2,0,1:T(8,128)(2,1)S(1)}, u32[]{:S(2)}, u32[]{:S(2)}) async-start(bf16[32,32,256]{2,0,1:T(8,128)(2,1)} %copy.41), calls=%async_computation.2 | async-start | bytes 1048576 | tf_op jit(solution)/shard_map/all_to_all | solution.py:81
where the time goes:
time: 410 us; the launch traced here: 409 us
  waiting for transfers between devices  232 us (57%)
  blocking collectives  59.5 us (15%)
  local copies, waits for them, and re-layouts  43 us (10%)
  starting transfers between devices  42.7 us (10%)
  matrix products  21 us (5%)
  other arithmetic  10.5 us (3%)
    all_to_all x1, waiting for transfers between devices, body(): lax.all_to_all(packed, 'zs', split_axis=0, concat_axis=0, tiled=True)  183 us
    all_to_all x1, blocking collectives, body(): lax.all_to_all(filtered, 'zs', split_axis=0, concat_axis=1, tiled=True)  59.5 us
    all_to_all x1, waiting for transfers between devices, body(): lax.all_to_all(z_major, 'zs', split_axis=1, concat_axis=0, tiled=True)  33.5 us
    dot_general x1, matrix products, body(): assembled = jnp.dot(placing, contrib, preferred_element_type=jnp.float32)  16.3 us
    all_to_all x1, starting transfers between devices, body(): lax.all_to_all(packed_ids, 'zs', split_axis=0, concat_axis=0, tiled=True)  15.5 us
    all_to_all x1, starting transfers between devices, body(): lax.all_to_all(packed, 'zs', split_axis=0, concat_axis=0, tiled=True)  11.2 us
    all_to_all x1, starting transfers between devices, body(): lax.all_to_all(z_major, 'zs', split_axis=1, concat_axis=0, tiled=True)  9.94 us
    slice x1, local copies, waits for them, and re-layouts, body(): arrived[:, 0].astype(jnp.float32) + arrived[:, 1].astype(jnp.float32)  8.97 us
  transfers between devices with their start and end apart: 5, of which 5 were waited for; matrix products, arithmetic and copies ran while one was open for 3% of the time, Pallas kernels for 0%

commit v1 on v0

--- a/solution.py
+++ b/solution.py
@@ -85,7 +85,9 @@
     windows = jnp.concatenate([pieces[:-2], pieces[1:-1], pieces[2:]], axis=1)
     filtered = jnp.einsum("ij,bjm->bim", z_matrix, windows, preferred_element_type=jnp.float32)
     filtered = filtered.reshape(line_length, 1, flat.shape[1])
-    returned = lax.all_to_all(filtered, "zs", split_axis=0, concat_axis=1, tiled=True)
+    parts = jnp.split(filtered, lax.axis_size("zs"), axis=0)
+    received = lax.all_to_all(jnp.stack(parts), "zs", 0, 0)
+    returned = jnp.concatenate(received, axis=1)
     smoothed = returned.reshape(CZ, CX, NY).transpose(1, 0, 2)
     return (gradient, smoothed)
 

time: 410 us -> 410 us (level)
  no operation moved by 1% of the time
where the time goes in v1:
time: 410 us; the launch traced here: 409 us
  waiting for transfers between devices  232 us (57%)
  blocking collectives  59.5 us (15%)
  starting transfers between devices  42.7 us (10%)
  local copies, waits for them, and re-layouts  42 us (10%)
  matrix products  21 us (5%)
  other arithmetic  10.5 us (3%)
    all_to_all x1, waiting for transfers between devices, body(): lax.all_to_all(packed, 'zs', split_axis=0, concat_axis=0, tiled=True)  183 us
    all_to_all x1, blocking collectives, body(): received = lax.all_to_all(jnp.stack(parts), 'zs', 0, 0)  59.5 us
    all_to_all x1, waiting for transfers between devices, body(): lax.all_to_all(z_major, 'zs', split_axis=1, concat_axis=0, tiled=True)  33.5 us
    dot_general x1, matrix products, body(): assembled = jnp.dot(placing, contrib, preferred_element_type=jnp.float32)  16.3 us
    all_to_all x1, starting transfers between devices, body(): lax.all_to_all(packed_ids, 'zs', split_axis=0, concat_axis=0, tiled=True)  15.5 us
    all_to_all x1, starting transfers between devices, body(): lax.all_to_all(packed, 'zs', split_axis=0, concat_axis=0, tiled=True)  11.2 us
    all_to_all x1, starting transfers between devices, body(): lax.all_to_all(z_major, 'zs', split_axis=1, concat_axis=0, tiled=True)  9.94 us
    slice x1, local copies, waits for them, and re-layouts, body(): arrived[:, 0].astype(jnp.float32) + arrived[:, 1].astype(jnp.float32)  8.97 us
  transfers between devices with their start and end apart: 5, of which 5 were waited for; matrix products, arithmetic and copies ran while one was open for 3% of the time, Pallas kernels for 0%

profile of v1, /device:TPU:26, one launch (start us, length us, event | category | flops | bytes accessed | tf_op | source)
XLA Modules:
  0.0 408.8 jit_solution(4977809685706745613)
XLA Ops:
  0.6 0.0 copy-start
  0.6 0.8 and_select_fusion.1
  1.5 0.1 fusion.14
  1.5 0.1 reduce_window_sum.11
  1.6 0.2 select_reduce_fusion.1
  1.8 0.7 fusion.20
  2.4 0.1 select_reduce_fusion
  2.5 0.7 all_to_all.25
  3.3 15.5 %all-to-all-start = ((s32[32,1,2]{2,1,0:T(1,128)}), s32[32,1,2]{2,1,0:T(1,128)S(1)}, u32[]{:S(2)}, u32[]{:S(2)}) async-start(s32[32,1,2]{2,1,0:T(1,128)} %bitcast.4), calls=%async_computation | async-start | bytes 32768 | tf_op jit(solution)/shard_map/all_to_all | solution.py:56
  18.7 0.0 copy-done
  18.8 3.3 convolution_convert_fusion
  22.1 7.6 %reshape.108 = bf16[32,2,32768]{2,1,0:T(2,128)(2,1)} reshape(bf16[64,32768]{1,0:T(8,128)(2,1)} %convolution_convert_fusion) | data formatting | bytes 8388608 | tf_op jit(solution)/shard_map/reshape | solution.py:52
  29.7 0.0 copy-start.2
  29.7 1.4 all-to-all-done
  31.1 11.2 %all-to-all-start.1 = ((bf16[32,2,32768]{2,1,0:T(2,128)(2,1)}), bf16[32,2,32768]{2,1,0:T(2,128)(2,1)}, u32[]{:S(2)}, u32[]{:S(2)}) async-start(bf16[32,2,32768]{2,1,0:T(2,128)(2,1)} %reshape.108), calls=%async_computation.1 | async-start | bytes 8388608 | tf_op jit(solution)/shard_map/all_to_all | solution.py:55
  42.3 0.0 copy-done.2
  42.3 0.1 multiply_reduce_fusion
  42.5 0.1 divide_convert_fusion
  42.6 0.1 copy.97
  42.7 183.2 %all-to-all-done.1 = bf16[32,2,32768]{2,1,0:T(2,128)(2,1)} async-done(((bf16[32,2,32768]{2,1,0:T(2,128)(2,1)}), bf16[32,2,32768]{2,1,0:T(2,128)(2,1)}, u32[]{:S(2)}, u32[]{:S(2)}) %all-to-all-start.1) | async-done | bytes 4194336 | tf_op jit(solution)/shard_map/all_to_all | solution.py:55
  225.9 9.0 %fusion.23 = (bf16[32,1,32768]{2,1,0:T(2,128)(2,1)S(1)}, bf16[32,1,32768]{2,1,0:T(2,128)(2,1)S(1)}) fusion(bf16[32,2,32768]{2,1,0:T(2,128)(2,1)} %all-to-all-done.1), kind=kLoop, calls=%fused_computation.125 | loop fusion | bytes 8388608 | tf_op jit(solution)/shard_map/slice | solution.py:58
  234.9 5.9 %fusion = bf16[32768,32]{0,1:T(8,128)(2,1)} fusion(bf16[32,1,32768]{2,1,0:T(2,128)(2,1)S(1)} %get-tuple-element.14, bf16[32,1,32768]{2,1,0:T(2,128)(2,1)S(1)} %get-tuple-element.13), kind=kLoop, calls=%fused_computation.4 | loop fusion | flops 4194304 | bytes 6291456 | tf_op jit(solution)/shard_map/dot_general | solution.py:63
  240.8 7.4 %copy.107 = bf16[32768,32]{1,0:T(8,128)(2,1)} copy(bf16[32768,32]{0,1:T(8,128)(2,1)} %fusion) | data formatting | bytes 4194304 | tf_op jit(solution)/shard_map/dot_general | solution.py:63
  248.1 16.3 %convolution_bitcast_fusion = f32[2,32,32,4,32]{2,3,4,1,0:T(4,128)} fusion(bf16[32,32,32,32,1]{3,2,1,0,4:T(8,128)(2,1)} %bitcast.212, s32[2,4]{1,0:T(2,128)S(1)} %multiply_add_fusion, s32[32]{0:T(128)S(1)} %slice_bitcast_fusion.36), kind=kOutput, calls=%fused_computation.3 | convolution fusion | flops 16777472 | bytes 3145888 | tf_op jit(solution)/shard_map/dot_general | solution.py:63
  264.4 6.3 %copy.101 = f32[2,32,32,4,32]{4,3,2,1,0:T(4,128)} copy(f32[2,32,32,4,32]{2,3,4,1,0:T(4,128)} %convolution_bitcast_fusion) | data formatting | bytes 2097152 | tf_op jit(solution)/shard_map/transpose | solution.py:64
  270.7 3.7 reshape.109
  274.4 0.0 copy-start.1
  274.4 1.0 convert_element_type.51
  275.5 3.0 collective-permute-start
  278.5 3.0 collective-permute-start.1
  281.6 0.2 reshape.110
  281.8 0.1 pad_slice_fusion.3
  281.9 0.1 copy.114
  282.0 0.3 reshape.113
  282.3 8.9 %collective-permute-done = bf16[64,32,128]{2,1,0:T(8,128)(2,1)} collective-permute-done((bf16[64,32,128]{2,1,0:T(8,128)(2,1)}, bf16[64,32,128]{2,1,0:T(8,128)(2,1)}, u32[]{:S(2)}, u32[]{:S(2)}) %collective-permute-start) | collective-permute-done | bytes 524320 | tf_op jit(solution)/shard_map/ppermute | solution.py:22
  291.2 4.9 %collective-permute-done.1 = bf16[64,32,128]{2,1,0:T(8,128)(2,1)} collective-permute-done((bf16[64,32,128]{2,1,0:T(8,128)(2,1)}, bf16[64,32,128]{2,1,0:T(8,128)(2,1)}, u32[]{:S(2)}, u32[]{:S(2)}) %collective-permute-start.1) | collective-permute-done | bytes 524320 | tf_op jit(solution)/shard_map/ppermute | solution.py:23
  296.1 1.5 pad_maximum_fusion
  297.6 0.6 fusion.10
  298.3 0.0 copy-done.1
  298.3 0.1 copy.113
  298.4 0.3 fusion.9
  298.7 0.2 copy.102
  298.9 0.2 reshape.114
  299.1 1.1 copy.103
  300.1 9.9 %all-to-all-start.2 = ((bf16[32,32,256]{2,0,1:T(8,128)(2,1)}), bf16[32,32,256]{2,0,1:T(8,128)(2,1)S(1)}, u32[]{:S(2)}, u32[]{:S(2)}) async-start(bf16[32,32,256]{2,0,1:T(8,128)(2,1)} %copy.103), calls=%async_computation.2 | async-start | bytes 1048576 | tf_op jit(solution)/shard_map/all_to_all | solution.py:81
  310.2 0.2 reshape.116
  310.3 33.5 %all-to-all-done.2 = bf16[32,32,256]{2,0,1:T(8,128)(2,1)S(1)} async-done(((bf16[32,32,256]{2,0,1:T(8,128)(2,1)}), bf16[32,32,256]{2,0,1:T(8,128)(2,1)S(1)}, u32[]{:S(2)}, u32[]{:S(2)}) %all-to-all-start.2) | async-done | bytes 524320 | tf_op jit(solution)/shard_map/all_to_all | solution.py:81
  343.9 0.1 pad_slice_fusion.1
  343.9 0.4 fusion.3
  344.8 59.5 %all_to_all.37 = f32[32,32,1,256]{3,1,2,0:T(8,128)S(1)} all-to-all(f32[32,32,1,256]{3,1,2,0:T(8,128)S(1)} %constant_dynamic-update-slice_fusion), channel_id=1, replica_groups=mesh['xb'=16,'zs'=32] {'zs'}, dimensions={0} | all-to-all | bytes 2097152 | tf_op jit(solution)/shard_map/all_to_all | solution.py:89
  404.3 0.6 copy.104
  404.9 1.1 reshape_reshape.3
  405.9 2.8 copy.105
  (45 shorter events, 0.3 us)
Async XLA Ops:
  0.6 18.1 %copy-start = (bf16[32,32768]{1,0:T(8,128)(2,1)S(1)}, bf16[32,32768]{1,0:T(8,128)(2,1)}, u32[]{:S(2)}) copy-start(bf16[32,32768]{1,0:T(8,128)(2,1)} %param.3) | copy-start | bytes 6291460
  3.3 27.9 %all-to-all-start = ((s32[32,1,2]{2,1,0:T(1,128)}), s32[32,1,2]{2,1,0:T(1,128)S(1)}, u32[]{:S(2)}, u32[]{:S(2)}) async-start(s32[32,1,2]{2,1,0:T(1,128)} %bitcast.4), calls=%async_computation | async-start | bytes 32768 | tf_op jit(solution)/shard_map/all_to_all | solution.py:56
  29.7 12.6 %copy-start.2 = (f32[3,129]{1,0:T(4,128)S(1)}, f32[3,129]{1,0:T(4,128)}, u32[]{:S(2)}) copy-start(f32[3,129]{1,0:T(4,128)} %param.5) | copy-start | bytes 4648
  31.1 194.8 %all-to-all-start.1 = ((bf16[32,2,32768]{2,1,0:T(2,128)(2,1)}), bf16[32,2,32768]{2,1,0:T(2,128)(2,1)}, u32[]{:S(2)}, u32[]{:S(2)}) async-start(bf16[32,2,32768]{2,1,0:T(2,128)(2,1)} %reshape.108), calls=%async_computation.1 | async-start | bytes 8388608 | tf_op jit(solution)/shard_map/all_to_all | solution.py:55
  274.4 23.8 %copy-start.1 = (f32[64,32,128]{2,1,0:T(8,128)}, f32[64,32,128]{2,1,0:T(8,128)S(1)}, u32[]{:S(2)}) copy-start(f32[64,32,128]{2,1,0:T(8,128)S(1)} %reshape.109) | copy-start | bytes 3145732
  275.5 15.7 %collective-permute-start = (bf16[64,32,128]{2,1,0:T(8,128)(2,1)}, bf16[64,32,128]{2,1,0:T(8,128)(2,1)}, u32[]{:S(2)}, u32[]{:S(2)}) collective-permute-start(bf16[64,32,128]{2,1,0:T(8,128)(2,1)} %convert_element_type.51), channel_id=1, source_target_pairs={{0,32},{32,64},{64,96},{96,128},{128,160},{160,192},{192,224},{224... | collective-permute-start | bytes 1572872 | tf_op jit(solution)/shard_map/ppermute | solution.py:22
  278.5 17.5 %collective-permute-start.1 = (bf16[64,32,128]{2,1,0:T(8,128)(2,1)}, bf16[64,32,128]{2,1,0:T(8,128)(2,1)}, u32[]{:S(2)}, u32[]{:S(2)}) collective-permute-start(bf16[64,32,128]{2,1,0:T(8,128)(2,1)} %convert_element_type.51), channel_id=1, source_target_pairs={{32,0},{64,32},{96,64},{128,96},{160,128},{192,160},{224,192},{256... | collective-permute-start | bytes 1572872 | tf_op jit(solution)/shard_map/ppermute | solution.py:23
  300.1 43.7 %all-to-all-start.2 = ((bf16[32,32,256]{2,0,1:T(8,128)(2,1)}), bf16[32,32,256]{2,0,1:T(8,128)(2,1)S(1)}, u32[]{:S(2)}, u32[]{:S(2)}) async-start(bf16[32,32,256]{2,0,1:T(8,128)(2,1)} %copy.103), calls=%async_computation.2 | async-start | bytes 1048576 | tf_op jit(solution)/shard_map/all_to_all | solution.py:81
